TPU v7x, 256 devices: a whole 4x4x8 slice. The times are simulated.
256 devices in a mesh: con: 4 (over z_hi), grid: 64 (over z_lo, y, x, core).
Axes of the slice: x: 4, y: 4, z: 8 (z_hi: 4, z_lo: 2; z = z_hi * 2 + z_lo), core: 2. Of those that a mesh axis runs over, the one named last changes fastest.
Arguments:
- velocity: bfloat16 [8, 2, 4096, 4096], P('con', None, 'grid'), may hold values from -6 to 6
- seed_adjoint: bfloat16 [8, 2, 4096, 4096], P('con', None, 'grid'), may hold values from -6 to 6
- land_mask: int32 [4096, 4096], P('grid'), may hold values from 0 to 2
- inv_x: bfloat16 [32, 128, 128], replicated, may hold values from -0.5 to 0.5
- inv_y: bfloat16 [32, 128, 128], replicated, may hold values from -0.5 to 0.5
- weights: float32 [8], P('con'), may hold values from 0.05 to 0.5
Outputs:
- velocity_adjoint: float32 [8, 2, 4096, 4096], P('con', None, 'grid')
Inputs may be any that keep to these rules, and one draw needn't show every extreme that they name: `land_mask`: 0 marks land, 1 a wet interior cell, 2 an open-boundary cell whose value is prescribed.
All inputs are finite; a program needn't handle non-finite values.
Results may differ from a plain program's by a relative error of at most 0.0039.
Values may be sent and summed in bfloat16 or wider, within the bound.
No kernel may reach another device: no remote copies, remote signals or barrier semaphores. Data moves between devices by JAX's collectives and lax.ppermute only.
A program may use at most 64 MiB of HBM per device.

v0:
```python
import jax
import jax.numpy as jnp
from jax import lax
from jax.sharding import PartitionSpec as P

BLK = 128


def local(velocity, seed_adjoint, land_mask, inv_x, inv_y, weights):
    nblocks = inv_x.shape[0]
    con_local = velocity.shape[0]
    cols_local = seed_adjoint.shape[2]
    full_side = seed_adjoint.shape[3]
    rows_local = velocity.shape[2]
    vel_float = velocity.astype(jnp.float32)
    weight_full = weights[:, None, None, None]
    local_squares = jnp.sum(weight_full * vel_float * vel_float, axis=(0, 1))
    squares = lax.psum(local_squares, "con")
    sea_bool = land_mask == 1
    sea_float = sea_bool.astype(jnp.float32)
    sea_turned = jnp.swapaxes(sea_bool, 0, 1).astype(jnp.bfloat16)
    blocks_x = seed_adjoint.reshape(con_local, 2, cols_local, nblocks, BLK)
    across = jnp.einsum("cpyki,kji->cpykj", blocks_x, inv_x, preferred_element_type=jnp.float32)
    across = across.astype(jnp.bfloat16).reshape(con_local, 2, cols_local, full_side)
    arrived = lax.all_to_all(across, "grid", split_axis=3, concat_axis=2, tiled=True)
    count = arrived.shape[0]
    masked = arrived * sea_turned[None, None]
    blocks_y = masked.reshape(count, 2, nblocks, BLK, rows_local)
    solved = jnp.einsum("cpkiu,kji->cpukj", blocks_y, inv_y, preferred_element_type=jnp.float32)
    rhs_adjoint = solved.reshape(count, 2, rows_local, nblocks * BLK)
    local_inner = jnp.sum(rhs_adjoint * vel_float, axis=(0, 1))
    inner = lax.psum(local_inner.astype(jnp.bfloat16), "con").astype(jnp.float32)
    speed = jnp.sqrt(0.25 + squares)
    first = -0.5 * sea_float * speed * rhs_adjoint
    second = -0.5 * sea_float * weight_full * vel_float * inner / speed
    return first + second


def solution(mesh):
    return jax.shard_map(
        local,
        mesh=mesh,
        in_specs=(
            P("con", None, "grid", None),
            P("con", None, "grid", None),
            P("grid", None),
            P(),
            P(),
            P("con"),
        ),
        out_specs=P("con", None, "grid", None),
        check_vma=False,
    )
```

profile of v0, /device:TPU:1, one launch (start us, length us, event | category | flops | bytes accessed | tf_op | source)
XLA Modules:
  0.0 237.2 jit_solution(3635252358337494409)
XLA Ops:
  6.5 0.0 copy-start
  6.5 1.6 copy-done
  8.1 3.3 %convert_bitcast_fusion = bf16[2,2,64,32,128]{4,2,1,0,3:T(8,128)(2,1)} fusion(bf16[32,128,128]{2,1,0:T(8,128)(2,1)} %param.9, bf16[2,2,64,4096]{3,2,1,0:T(8,128)(2,1)S(1)} %copy-done), kind=kOutput, calls=%fused_computation.16 | convolution fusion | flops 269484032 | bytes 5242880 | tf_op jit(solution)/shard_map/cpyki,kji->cpykj/dot_general | solution.py:23
  11.4 10.0 %copy.22 = bf16[2,2,64,32,128]{2,1,0,4,3:T(2,128)(2,1)} copy(bf16[2,2,64,32,128]{4,2,1,0,3:T(8,128)(2,1)} %convert_bitcast_fusion) | data formatting | bytes 4194304 | tf_op jit(solution)/shard_map/reshape | solution.py:24
  21.4 9.8 %reshape.31 = bf16[64,2,8192]{2,1,0:T(2,128)(2,1)} reshape(bf16[4096,2,2,64]{3,2,1,0:T(2,128)(2,1)} %bitcast.46) | data formatting | bytes 4194304
  31.3 10.5 %all-to-all-start = ((bf16[64,2,8192]{2,1,0:T(2,128)(2,1)}), bf16[64,2,8192]{2,1,0:T(2,128)(2,1)}, u32[]{:S(2)}, u32[]{:S(2)}) async-start(bf16[64,2,8192]{2,1,0:T(2,128)(2,1)} %reshape.31), calls=%async_computation | async-start | bytes 4194304 | tf_op jit(solution)/shard_map/all_to_all | solution.py:25
  41.8 0.2 all-reduce.5.cloned.1.call-start
  42.0 1.4 broadcast_select_fusion
  43.4 0.1 convert_bitcast_fusion.1
  43.6 0.9 copy.26
  44.5 24.8 %all-to-all-done = bf16[64,2,8192]{2,1,0:T(2,128)(2,1)} async-done(((bf16[64,2,8192]{2,1,0:T(2,128)(2,1)}), bf16[64,2,8192]{2,1,0:T(2,128)(2,1)}, u32[]{:S(2)}, u32[]{:S(2)}) %all-to-all-start) | async-done | bytes 2097184 | tf_op jit(solution)/shard_map/all_to_all | solution.py:25
  69.2 9.8 %reshape.32 = bf16[4096,2,2,64]{3,2,1,0:T(2,128)(2,1)} reshape(bf16[64,2,8192]{2,1,0:T(2,128)(2,1)} %all-to-all-done) | data formatting | bytes 4194304
  79.0 6.8 %copy.38 = bf16[2,2,64,64,64]{2,3,4,1,0:T(8,128)(2,1)} copy(bf16[2,2,64,64,64]{2,1,0,4,3:T(2,128)(2,1)} %bitcast.47) | data formatting | bytes 4194304 | tf_op jit(solution)/shard_map/all_to_all | solution.py:25
  85.8 6.2 %all_to_all.16 = bf16[2,2,32,128,64]{3,2,4,1,0:T(8,128)(2,1)} reshape(bf16[2,2,64,64,64]{3,2,4,1,0:T(8,128)(2,1)} %bitcast.48) | data formatting | bytes 4194304 | tf_op jit(solution)/shard_map/all_to_all | solution.py:25
  92.0 0.0 copy-start.4
  92.0 2.0 broadcast_multiply_fusion.1
  94.0 0.0 copy-done.4
  94.0 1.2 convolution_bitcast_fusion
  95.2 0.4 copy-done.3
  95.6 0.0 copy-done.5
  95.6 2.4 %fusion.4 = (bf16[64,4096]{1,0:T(8,128)(2,1)}, f32[64,4096]{1,0:T(8,128)}) fusion(bf16[2,2,64,4096]{3,2,1,0:T(8,128)(2,1)S(1)} %copy-done.3, f32[32,2,2,8,8,128]{5,4,3,2,1,0:T(8,128)S(1)} %convolution_bitcast_fusion, f32[2]{0:T(128)S(1)} %copy-done.5), kind=kLoop, calls=%fused_computation.8 | loop fusion | flops 5767168 | bytes 7864328 | tf_op jit(solution)/shard_map/reduce_sum | solution.py:31
  98.0 0.0 copy-done.1
  98.1 0.0 all-reduce.5.cloned.1.call-update
  98.1 0.0 all-reduce.3.cloned.1.call-start
  98.1 0.7 all-reduce.3.cloned.1.call-update
  98.8 1.6 broadcast_multiply_fusion
  100.5 52.3 %all-reduce.5.cloned.1.call-done = bf16[64,4096]{1,0:T(8,128)(2,1)} async-done(((bf16[64,4096]{1,0:T(8,128)(2,1)}), bf16[64,4096]{1,0:T(8,128)(2,1)}) %all-reduce.5.cloned.1.call-update) | async-done | bytes 524304 | tf_op jit(solution)/shard_map/psum | solution.py:32
  152.8 1.1 convert_element_type.25
  153.9 68.7 %all-reduce.3.cloned.1.call-done = f32[64,4096]{1,0:T(8,128)} async-done(((f32[64,4096]{1,0:T(8,128)}), f32[64,4096]{1,0:T(8,128)}) %all-reduce.3.cloned.1.call-update) | async-done | bytes 1048592 | tf_op jit(solution)/shard_map/psum | solution.py:18
  222.6 1.8 fusion.13
  224.4 0.1 copy-done.2
  224.5 5.9 %fusion.3 = f32[2,2,64,4096]{3,2,1,0:T(8,128)} fusion(bf16[2,2,64,4096]{3,2,1,0:T(8,128)(2,1)} %param.6, f32[32,2,2,8,8,128]{5,4,3,2,1,0:T(8,128)} %copy-done.1, f32[64,4096]{1,0:T(8,128)S(1)} %get-tuple-element.10, f32[64,4096]{1,0:T(8,128)S(1)} %convert_element_type.25, f32[2,64,4096]{2,1,0:T(8,128)S(1)} %copy-done.2, f32[64,4096]{1,0:T(8,128)S(1)} %get-tuple-element.9), kind=kLoop, calls=%fused_computation.7 | loop fusion | flops 6291456 | bytes 15728640 | tf_op jit(solution)/shard_map/add | solution.py:36
  (4 shorter events, 0.0 us)
Async XLA Ops:
  6.5 1.6 copy-start
  31.3 38.0 %all-to-all-start = ((bf16[64,2,8192]{2,1,0:T(2,128)(2,1)}), bf16[64,2,8192]{2,1,0:T(2,128)(2,1)}, u32[]{:S(2)}, u32[]{:S(2)}) async-start(bf16[64,2,8192]{2,1,0:T(2,128)(2,1)} %reshape.31), calls=%async_computation | async-start | bytes 4194304 | tf_op jit(solution)/shard_map/all_to_all | solution.py:25
  41.8 111.0 %all-reduce.5.cloned.1.call-start = ((), (), s32[]{:S(2)}) async-start(), calls=%async_computation.2 | async-start | bytes 1048576 | tf_op jit(solution)/shard_map/psum | solution.py:32
  92.0 2.0 copy-start.4
  94.0 1.6 copy-start.3
  94.0 1.6 copy-start.5
  95.6 2.4 %copy-start.1 = (f32[32,2,2,8,8,128]{5,4,3,2,1,0:T(8,128)}, f32[32,2,2,8,8,128]{5,4,3,2,1,0:T(8,128)S(1)}, u32[]{:S(2)}) copy-start(f32[32,2,2,8,8,128]{5,4,3,2,1,0:T(8,128)S(1)} %convolution_bitcast_fusion) | copy-start | bytes 12582916
  98.1 124.5 %all-reduce.3.cloned.1.call-start = ((), (), s32[]{:S(2)}) async-start(), calls=%async_computation.1 | async-start | bytes 2097152 | tf_op jit(solution)/shard_map/psum | solution.py:18
  222.6 1.9 copy-start.2
Sparse Core Ops, SparseCore 0:
  98.2 54.5 all-reduce.4
  155.4 67.1 all-reduce.2
where the time goes:
time: 238 us; the launch traced here: 237 us
  waiting for transfers between devices  146 us (61%)
  local copies, waits for them, and re-layouts  45.7 us (19%)
  other arithmetic  16.3 us (7%)
  between operations  13.5 us (6%)
  starting transfers between devices  10.8 us (5%)
  matrix products  4.45 us (2%)
    psum x1, waiting for transfers between devices, local(): squares = lax.psum(local_squares, 'con')  68.7 us
    psum x1, waiting for transfers between devices, local(): lax.psum(local_inner.astype(jnp.bfloat16), 'con').astype(jnp.float32)  52.3 us
    all_to_all x1, waiting for transfers between devices, local(): lax.all_to_all(across, 'grid', split_axis=3, concat_axis=2, tiled=True)  24.8 us
    unnamed x15, local copies, waits for them, and re-layouts  22.7 us
    all_to_all x2, local copies, waits for them, and re-layouts, local(): lax.all_to_all(across, 'grid', split_axis=3, concat_axis=2, tiled=True)  13 us
    all_to_all x1, starting transfers between devices, local(): lax.all_to_all(across, 'grid', split_axis=3, concat_axis=2, tiled=True)  10.5 us
    reshape x1, local copies, waits for them, and re-layouts, local(): across.astype(jnp.bfloat16).reshape(con_local, 2, cols_local, full_side)  10 us
    add x1, other arithmetic, local(): return first + second  5.88 us
  transfers between devices with their start and end apart: 3, of which 3 were waited for; matrix products, arithmetic and copies ran while one was open for 2% of the time, Pallas kernels for 0%

commit v1 on v0

--- a/solution.py
+++ b/solution.py
@@ -1,9 +1,18 @@
+import functools
 import jax
 import jax.numpy as jnp
 from jax import lax
 from jax.sharding import PartitionSpec as P
 
 BLK = 128
+
+
+def values_lift(frame, row_axis):
+    block_out = jnp.sum(lax.all_gather(frame, row_axis), axis=0)
+    return block_out
+
+
+render_screen_here = functools.partial(values_lift, row_axis="con")
 
 
 def local(velocity, seed_adjoint, land_mask, inv_x, inv_y, weights):
@@ -15,7 +24,7 @@
     vel_float = velocity.astype(jnp.float32)
     weight_full = weights[:, None, None, None]
     local_squares = jnp.sum(weight_full * vel_float * vel_float, axis=(0, 1))
-    squares = lax.psum(local_squares, "con")
+    squares = render_screen_here(local_squares)
     sea_bool = land_mask == 1
     sea_float = sea_bool.astype(jnp.float32)
     sea_turned = jnp.swapaxes(sea_bool, 0, 1).astype(jnp.bfloat16)

time: 238 us -> 259 us (1.088)
  the two profiles are of different devices: /device:TPU:1 before, /device:TPU:36 now
where the time goes in v1:
time: 259 us; the launch traced here: 258 us
  waiting for transfers between devices  165 us (64%)
  local copies, waits for them, and re-layouts  47 us (18%)
  other arithmetic  18.6 us (7%)
  between operations  13.5 us (5%)
  starting transfers between devices  9.46 us (4%)
  matrix products  4.47 us (2%)
    all_gather x1, waiting for transfers between devices, values_lift(): block_out = jnp.sum(lax.all_gather(frame, row_axis), axis=0)  85.9 us
    psum x1, waiting for transfers between devices, local(): lax.psum(local_inner.astype(jnp.bfloat16), 'con').astype(jnp.float32)  53.3 us
    all_to_all x1, waiting for transfers between devices, local(): lax.all_to_all(across, 'grid', split_axis=3, concat_axis=2, tiled=True)  24.6 us
    unnamed x17, local copies, waits for them, and re-layouts  24 us
    all_to_all x2, local copies, waits for them, and re-layouts, local(): lax.all_to_all(across, 'grid', split_axis=3, concat_axis=2, tiled=True)  13 us
    reshape x1, local copies, waits for them, and re-layouts, local(): across.astype(jnp.bfloat16).reshape(con_local, 2, cols_local, full_side)  10 us
    all_to_all x1, starting transfers between devices, local(): lax.all_to_all(across, 'grid', split_axis=3, concat_axis=2, tiled=True)  9.2 us
    add x1, other arithmetic, local(): return first + second  5.92 us
  transfers between devices with their start and end apart: 3, of which 3 were waited for; matrix products, arithmetic and copies ran while one was open for 2% of the time, Pallas kernels for 0%

profile of v1, /device:TPU:36, one launch (start us, length us, event | category | flops | bytes accessed | tf_op | source)
XLA Modules:
  0.0 257.6 jit_solution(4225432053347429878)
XLA Ops:
  6.5 1.6 copy-done
  8.1 3.3 %convert_bitcast_fusion = bf16[2,2,64,32,128]{4,2,1,0,3:T(8,128)(2,1)} fusion(bf16[32,128,128]{2,1,0:T(8,128)(2,1)} %param.9, bf16[2,2,64,4096]{3,2,1,0:T(8,128)(2,1)S(1)} %copy-done), kind=kOutput, calls=%fused_computation.16 | convolution fusion | flops 269484032 | bytes 5242880 | tf_op jit(solution)/shard_map/cpyki,kji->cpykj/dot_general | solution.py:32
  11.4 10.0 %copy.28 = bf16[2,2,64,32,128]{2,1,0,4,3:T(2,128)(2,1)} copy(bf16[2,2,64,32,128]{4,2,1,0,3:T(8,128)(2,1)} %convert_bitcast_fusion) | data formatting | bytes 4194304 | tf_op jit(solution)/shard_map/reshape | solution.py:33
  21.4 9.8 %reshape.35 = bf16[64,2,8192]{2,1,0:T(2,128)(2,1)} reshape(bf16[4096,2,2,64]{3,2,1,0:T(2,128)(2,1)} %bitcast.47) | data formatting | bytes 4194304
  31.3 9.2 %all-to-all-start = ((bf16[64,2,8192]{2,1,0:T(2,128)(2,1)}), bf16[64,2,8192]{2,1,0:T(2,128)(2,1)}, u32[]{:S(2)}, u32[]{:S(2)}) async-start(bf16[64,2,8192]{2,1,0:T(2,128)(2,1)} %reshape.35), calls=%async_computation | async-start | bytes 4194304 | tf_op jit(solution)/shard_map/all_to_all | solution.py:34
  40.5 0.2 all-reduce.2.cloned.1.call-start
  40.7 1.4 broadcast_select_fusion
  42.1 0.1 convert_bitcast_fusion.1
  42.2 0.9 copy.32
  43.2 24.6 %all-to-all-done = bf16[64,2,8192]{2,1,0:T(2,128)(2,1)} async-done(((bf16[64,2,8192]{2,1,0:T(2,128)(2,1)}), bf16[64,2,8192]{2,1,0:T(2,128)(2,1)}, u32[]{:S(2)}, u32[]{:S(2)}) %all-to-all-start) | async-done | bytes 2097184 | tf_op jit(solution)/shard_map/all_to_all | solution.py:34
  67.8 9.8 %reshape.36 = bf16[4096,2,2,64]{3,2,1,0:T(2,128)(2,1)} reshape(bf16[64,2,8192]{2,1,0:T(2,128)(2,1)} %all-to-all-done) | data formatting | bytes 4194304
  77.6 6.8 %copy.44 = bf16[2,2,64,64,64]{2,3,4,1,0:T(8,128)(2,1)} copy(bf16[2,2,64,64,64]{2,1,0,4,3:T(2,128)(2,1)} %bitcast.48) | data formatting | bytes 4194304 | tf_op jit(solution)/shard_map/all_to_all | solution.py:34
  84.4 6.2 %all_to_all.16 = bf16[2,2,32,128,64]{3,2,4,1,0:T(8,128)(2,1)} reshape(bf16[2,2,64,64,64]{3,2,4,1,0:T(8,128)(2,1)} %bitcast.49) | data formatting | bytes 4194304 | tf_op jit(solution)/shard_map/all_to_all | solution.py:34
  90.6 2.0 broadcast_multiply_fusion.1
  92.6 0.0 copy-done.5
  92.6 1.2 convolution_bitcast_fusion
  93.8 0.4 copy-done.3
  94.2 2.6 fusion.4
  96.8 0.0 all-reduce.2.cloned.1.call-update
  96.8 0.0 all-gather.3.cloned.1.call-start
  96.9 0.7 all-gather.3.cloned.1.call-update
  97.6 1.6 broadcast_multiply_fusion
  99.2 53.3 %all-reduce.2.cloned.1.call-done = bf16[64,4096]{1,0:T(8,128)(2,1)} async-done(((bf16[64,4096]{1,0:T(8,128)(2,1)}), bf16[64,4096]{1,0:T(8,128)(2,1)}) %all-reduce.2.cloned.1.call-update) | async-done | bytes 524304 | tf_op jit(solution)/shard_map/psum | solution.py:41
  152.5 2.1 convert_element_type.25
  154.5 85.9 %all-gather.3.cloned.1.call-done = f32[256,4096]{1,0:T(8,128)} async-done(((f32[64,4096]{1,0:T(8,128)}), f32[256,4096]{1,0:T(8,128)}) %all-gather.3.cloned.1.call-update) | async-done | bytes 4194320 | tf_op jit(solution)/shard_map/all_gather | solution.py:11
  240.5 2.5 reduce_sum.28
  243.0 0.0 copy-start.2
  243.0 0.0 copy-start.4
  243.0 0.4 fusion.13
  243.4 1.2 copy-done.2
  244.6 0.3 copy-done.4
  244.8 5.9 %fusion.3 = f32[2,2,64,4096]{3,2,1,0:T(8,128)} fusion(bf16[2,2,64,4096]{3,2,1,0:T(8,128)(2,1)} %param.6, f32[32,2,2,8,8,128]{5,4,3,2,1,0:T(8,128)} %copy-done.1, f32[64,4096]{1,0:T(8,128)S(1)} %get-tuple-element.10, f32[64,4096]{1,0:T(8,128)S(1)} %copy-done.4, f32[2,64,4096]{2,1,0:T(8,128)S(1)} %copy-done.2, f32[64,4096]{1,0:T(8,128)S(1)} %get-tuple-element.9), kind=kLoop, calls=%fused_computation.7 | loop fusion | flops 6291456 | bytes 15728640 | tf_op jit(solution)/shard_map/add | solution.py:45
  (7 shorter events, 0.0 us)
Async XLA Ops:
  6.5 1.6 copy-start
  31.3 36.5 %all-to-all-start = ((bf16[64,2,8192]{2,1,0:T(2,128)(2,1)}), bf16[64,2,8192]{2,1,0:T(2,128)(2,1)}, u32[]{:S(2)}, u32[]{:S(2)}) async-start(bf16[64,2,8192]{2,1,0:T(2,128)(2,1)} %reshape.35), calls=%async_computation | async-start | bytes 4194304 | tf_op jit(solution)/shard_map/all_to_all | solution.py:34
  40.5 112.0 %all-reduce.2.cloned.1.call-start = ((), (), s32[]{:S(2)}) async-start(), calls=%async_computation.1 | async-start | bytes 1048576 | tf_op jit(solution)/shard_map/psum | solution.py:41
  90.6 2.0 copy-start.5
  92.6 1.6 copy-start.3
  92.6 1.6 copy-start.6
  94.2 2.6 copy-start.1
  96.8 143.6 %all-gather.3.cloned.1.call-start = ((), (), s32[]{:S(2)}) async-start(), calls=%async_computation.2 | async-start | bytes 5242880 | tf_op jit(solution)/shard_map/all_gather | solution.py:11
  243.0 1.6 copy-start.2
  243.0 1.8 copy-start.4
Sparse Core Ops, SparseCore 0:
  96.9 55.4 all-reduce.1
  154.3 86.1 all-gather.2
